TPU v7x, 32 devices: a whole 2x2x4 slice. The times are simulated.
32 devices in a mesh: groups: 2 (over x), seq: 16 (over z, y, core).
Axes of the slice: x: 2, y: 2, z: 4, core: 2. Of those that a mesh axis runs over, the one named last changes fastest.
Arguments:
- query: bfloat16 [4096, 1024], P(('groups', 'seq')), parts along dimension 0, as said below
- keys: bfloat16 [4096, 1024], P(('groups', 'seq')), parts along dimension 0, as said below
- values: bfloat16 [4096, 1024], P(('groups', 'seq')), parts along dimension 0, may hold values from -6 to 6
- out_weight: bfloat16 [1024, 2048], P('seq'), may hold values from -0.1875 to 0.1875
- grad_out: bfloat16 [4096, 2048], P(('groups', 'seq')), parts along dimension 0, may hold values from -6 to 6
- global_blocks: int32 [4], P('groups'), parts along dimension 0, may hold values from 0 to 15
- random_blocks: int32 [32, 3], P(('groups', 'seq')), parts along dimension 0, may hold values from 0 to 15, as said below
Outputs:
- layer_out: bfloat16 [4096, 2048], P(('groups', 'seq')), parts along dimension 0
- grad_query: bfloat16 [4096, 1024], P(('groups', 'seq')), parts along dimension 0
- grad_keys: bfloat16 [4096, 1024], P(('groups', 'seq')), parts along dimension 0
- grad_values: bfloat16 [4096, 1024], P(('groups', 'seq')), parts along dimension 0
- grad_weight: float32 [2048, 2048], P(('groups', 'seq')), parts along dimension 0
There are 2 independent parts, one for each index of `groups`. A program takes and returns all parts, laid end to end along the dimension named above; an argument that names none is the same for every part. Nothing has to cross between parts.
Inputs may be any that keep to these rules, and one draw needn't show every extreme that they name: `random_blocks`: random block r of query block b lies on the device that holds b or on a device beside it: it is at least max(b - 1, 0) * 1 and below min(b + 2, 16). `query`: entries lie between -12 and 12. `keys`: entries lie between -6 and 6.
All inputs are finite; a program needn't handle non-finite values.
Results may differ from a plain program's by a relative error of at most 0.012.
Values may be sent and summed in bfloat16 or wider, within the bound.
No kernel may reach another device: no remote copies, remote signals or barrier semaphores. Data moves between devices by JAX's collectives and lax.ppermute only.
A program may use at most 128 MiB of HBM per device.

v0:
```python
import math
import jax
import jax.numpy as jnp
from jax import lax
from jax.sharding import PartitionSpec as P

H = 8
BLK = 128
NEG_FILL = -1e30


def extended_2(shard, sides, width):
    for axis, dim in sides:
        count, length = (lax.axis_size(axis), shard.shape[dim])
        up = [(i, (i + 1) % count) for i in range(count - 1)]
        down = [(j, i) for i, j in up]
        last = lax.slice_in_dim(shard, length - width, length, axis=dim)
        initial = lax.slice_in_dim(shard, 0, width, axis=dim)
        before = lax.ppermute(last, axis, up)
        after = lax.ppermute(initial, axis, down)
        shard = jnp.concatenate([before, shard, after], axis=dim)
    return shard


def spread(shard, axis, root):
    mine = lax.axis_index(axis) == root
    return lax.psum(jnp.where(mine, shard, jnp.zeros_like(shard)), axis)


def window_and_random(random_rows, device, blocks_dev, total_blocks):
    local_ids = jnp.arange(blocks_dev, dtype=jnp.int32)
    global_ids = device * blocks_dev + local_ids
    offsets = jnp.array([-1, 0, 1], dtype=jnp.int32)
    neighbour_ids = global_ids[:, None] + offsets[None, :]
    window_index = local_ids[:, None] + blocks_dev + offsets[None, :]
    window_live = (neighbour_ids >= 0) & (neighbour_ids < total_blocks)
    random_index = random_rows - (device - 1) * blocks_dev
    ext_index = jnp.concatenate([window_index, random_index], axis=1)
    live_local = jnp.concatenate(
        [window_live, jnp.ones(random_rows.shape, dtype=jnp.bool_)], axis=1
    )
    return (ext_index, live_local)


def choose_blocks(extended, global_kv, ext_index, live_local, blocks_dev):
    feature_count = extended.shape[2]
    ext_blocks = extended.reshape(2, 3 * blocks_dev, BLK, feature_count)
    local_sel = jnp.take(ext_blocks, ext_index, axis=1)
    global_count = global_kv.shape[0]
    global_sel = jnp.swapaxes(global_kv, 0, 1)[:, None]
    chosen = jnp.concatenate([local_sel, global_sel], axis=2)
    listed = chosen.shape[2]
    chosen = chosen.reshape(2, blocks_dev, listed * BLK, H, feature_count // H)
    live = jnp.concatenate(
        [live_local, jnp.ones((blocks_dev, global_count), dtype=jnp.bool_)], axis=1
    )
    live_rows = jnp.repeat(live, BLK, axis=1)
    return (chosen[0], chosen[1], live_rows)


def attend_blocks(query_blocks, chosen_keys, chosen_values, live_rows):
    score_scale = 1.0 / math.sqrt(query_blocks.shape[-1])
    scores = (
        jnp.einsum("qihd,qjhd->qhij", query_blocks, chosen_keys, preferred_element_type=jnp.float32)
        * score_scale
    )
    scores = jnp.where(live_rows[:, None, None, :], scores, NEG_FILL)
    row_top = jnp.max(scores, axis=-1, keepdims=True)
    raised = jnp.exp(scores - row_top)
    soft_weights = raised / jnp.sum(raised, axis=-1, keepdims=True)
    rounded_weights = soft_weights.astype(jnp.bfloat16)
    mixed_out = jnp.einsum(
        "qhij,qjhd->qihd", rounded_weights, chosen_values, preferred_element_type=jnp.float32
    )
    return (soft_weights, rounded_weights, mixed_out.astype(jnp.bfloat16))


def attend_backward(
    query_blocks, chosen_keys, chosen_values, soft_weights, rounded_weights, upstream_blocks
):
    score_scale = 1.0 / math.sqrt(query_blocks.shape[-1])
    grad_chosen_values = jnp.einsum(
        "qhij,qihd->qjhd", rounded_weights, upstream_blocks, preferred_element_type=jnp.float32
    )
    grad_weights = jnp.einsum(
        "qihd,qjhd->qhij", upstream_blocks, chosen_values, preferred_element_type=jnp.float32
    )
    row_delta = jnp.sum(soft_weights * grad_weights, axis=-1, keepdims=True)
    grad_scores = (score_scale * soft_weights * (grad_weights - row_delta)).astype(jnp.bfloat16)
    grad_query_blocks = jnp.einsum(
        "qhij,qjhd->qihd", grad_scores, chosen_keys, preferred_element_type=jnp.float32
    )
    grad_chosen_keys = jnp.einsum(
        "qhij,qihd->qjhd", grad_scores, query_blocks, preferred_element_type=jnp.float32
    )
    return (grad_query_blocks, grad_chosen_keys, grad_chosen_values)


def fold_gradients(grad_chosen_keys, grad_chosen_values, ext_index, blocks_dev):
    stacked = jnp.stack([grad_chosen_keys, grad_chosen_values])
    listed_local = ext_index.shape[1]
    feature_count = stacked.shape[3] * stacked.shape[4]
    stacked = stacked.reshape(2, blocks_dev, -1, BLK * feature_count)
    local_part = stacked[:, :, :listed_local].reshape(
        2, blocks_dev * listed_local, BLK * feature_count
    )
    one_hot = (
        ext_index.reshape(-1)[:, None] == jnp.arange(3 * blocks_dev, dtype=jnp.int32)[None, :]
    ).astype(jnp.float32)
    grad_ext = jnp.einsum("sj,ksx->kjx", one_hot, local_part, precision=lax.Precision.HIGHEST)
    grad_ext = grad_ext.reshape(2, 3 * blocks_dev * BLK, feature_count)
    grad_global = jnp.sum(stacked[:, :, listed_local:], axis=1).reshape(2, -1, BLK, feature_count)
    return (grad_ext, grad_global)


def local(query, keys, values, out_weight, grad_out, global_blocks, random_blocks):
    tok_rows = query.shape[0]
    feature_count = query.shape[1]
    blocks_dev = tok_rows // BLK
    device = lax.axis_index("seq")
    total_blocks = blocks_dev * lax.axis_size("seq")
    paired = jnp.stack([keys, values])
    extended = extended_2(paired, (("seq", 1),), tok_rows)
    fetched = []
    for global_slot in range(global_blocks.shape[0]):
        block_id = global_blocks[global_slot]
        owner_index = block_id // blocks_dev
        fetched.append(spread(paired, "seq", owner_index))
    global_kv = jnp.stack(fetched)
    ext_index, live_local = window_and_random(random_blocks, device, blocks_dev, total_blocks)
    chosen_keys, chosen_values, live_rows = choose_blocks(
        extended, global_kv, ext_index, live_local, blocks_dev
    )
    query_blocks = query.reshape(blocks_dev, BLK, H, feature_count // H)
    soft_weights, rounded_weights, mixed_out = attend_blocks(
        query_blocks, chosen_keys, chosen_values, live_rows
    )
    attn_out = mixed_out.reshape(tok_rows, feature_count)
    columns = attn_out
    layer_sum = jnp.dot(
        columns,
        lax.all_gather(out_weight, "seq", axis=0, tiled=True),
        preferred_element_type=jnp.float32,
    )
    upstream_sum = lax.dot_general(
        grad_out,
        lax.all_gather(out_weight, "seq", axis=0, tiled=True),
        (((1,), (1,)), ((), ())),
        preferred_element_type=jnp.float32,
    )
    layer_out = layer_sum.astype(jnp.bfloat16)
    upstream_blocks = upstream_sum.astype(jnp.bfloat16).reshape(
        blocks_dev, BLK, H, feature_count // H
    )
    columns = attn_out
    grad_weight = lax.psum_scatter(
        lax.dot_general(
            columns, grad_out, (((0,), (0,)), ((), ())), preferred_element_type=jnp.float32
        ),
        "seq",
        scatter_dimension=0,
        tiled=True,
    )
    grad_query_blocks, grad_chosen_keys, grad_chosen_values = attend_backward(
        query_blocks, chosen_keys, chosen_values, soft_weights, rounded_weights, upstream_blocks
    )
    grad_ext, grad_global = fold_gradients(
        grad_chosen_keys, grad_chosen_values, ext_index, blocks_dev
    )
    rim_grads = jnp.concatenate(
        [grad_ext[:, :tok_rows], grad_ext[:, 2 * tok_rows :]], axis=1
    ).astype(jnp.bfloat16)
    arrived = extended_2(rim_grads, (("seq", 1),), tok_rows)
    global_total = lax.psum(grad_global, "seq")
    owned_mask = (
        global_blocks[:, None]
        == device * blocks_dev + jnp.arange(blocks_dev, dtype=jnp.int32)[None, :]
    ).astype(jnp.float32)
    owned_sum = jnp.einsum(
        "gj,kgx->kjx",
        owned_mask,
        global_total.reshape(2, owned_mask.shape[0], -1),
        precision=lax.Precision.HIGHEST,
    )
    grad_paired = grad_ext[:, tok_rows : 2 * tok_rows] + arrived[:, :tok_rows].astype(jnp.float32)
    grad_paired = grad_paired + arrived[:, 3 * tok_rows :].astype(jnp.float32)
    grad_paired = grad_paired + owned_sum.reshape(2, tok_rows, feature_count)
    grad_paired = grad_paired.astype(jnp.bfloat16)
    grad_query = grad_query_blocks.reshape(tok_rows, feature_count).astype(jnp.bfloat16)
    return (layer_out, grad_query, grad_paired[0], grad_paired[1], grad_weight)


def solution(mesh):
    placed = (
        P(("groups", "seq"), None),
        P(("groups", "seq"), None),
        P(("groups", "seq"), None),
        P("seq", None),
        P(("groups", "seq"), None),
        P("groups"),
        P(("groups", "seq"), None),
    )
    return jax.shard_map(
        local,
        mesh=mesh,
        in_specs=placed,
        out_specs=(
            P(("groups", "seq"), None),
            P(("groups", "seq"), None),
            P(("groups", "seq"), None),
            P(("groups", "seq"), None),
            P(("groups", "seq"), None),
        ),
        check_vma=False,
    )
```

profile of v0, /device:TPU:0, one launch (start us, length us, event | category | flops | bytes accessed | tf_op | source)
XLA Modules:
  0.0 429.1 jit_solution(10546698557166395422)
XLA Ops:
  7.3 1.4 fusion.36
  10.0 2.1 select_bitcast_fusion.1
  12.1 0.7 all-gather.2.cloned.1.call-update
  12.9 1.3 collective-permute-start.1
  14.2 3.8 collective-permute-start
  18.4 0.5 collective-permute-done
  18.9 1.2 pad_maximum_fusion.2
  20.0 2.5 gather_fusion
  22.5 89.4 %all-reduce.6.cloned.1.call-done = (bf16[1,2,128,1024]{3,2,1,0:T(8,128)(2,1)}, bf16[1,2,128,1024]{3,2,1,0:T(8,128)(2,1)}) async-done(((bf16[1,2,128,1024]{3,2,1,0:T(8,128)(2,1)}, bf16[1,2,128,1024]{3,2,1,0:T(8,128)(2,1)}), (bf16[1,2,128,1024]{3,2,1,0:T(8,128)(2,1)}, bf16[1,2,128,1024]{3,2,1,0:T(8,128)(2,1)})) %all-reduce.6.cloned.1.call-update) | async-done | bytes 1048592 | tf_op jit(solution)/shard_map/psum | solution.py:27
  111.9 1.3 maximum_bitcast_fusion.2
  113.2 2.3 bitcast_select_fusion
  115.5 1.6 pad_maximum_fusion.1
  117.1 0.6 copy.57
  117.7 3.0 copy.52
  120.7 3.6 copy.58
  124.3 3.3 copy.34
  127.6 0.8 fusion.22
  128.4 3.4 fusion.37
  131.8 32.2 %all-gather.2.cloned.1.call-done = bf16[1024,2048]{1,0:T(8,128)(2,1)} async-done(((bf16[64,2048]{1,0:T(8,128)(2,1)}), bf16[1024,2048]{1,0:T(8,128)(2,1)}) %all-gather.2.cloned.1.call-update) | async-done | bytes 4194320 | tf_op jit(solution)/shard_map/all_gather | solution.py:142
  164.0 3.7 convolution_convert_fusion.3
  167.9 5.0 %convolution_bitcast_fusion.1 = f32[1,1024,8,128]{1,3,2,0:T(8,128)} fusion(bf16[128,8,128]{0,2,1:T(8,128)(2,1)S(1)} %bitcast.154, f32[8,128,1024]{1,2,0:T(8,128)} %get-tuple-element.29, f32[8,128]{1,0:T(8,128)S(1)} %get-tuple-element.28), kind=kOutput, calls=%fused_computation.19 | convolution fusion | flops 270532608 | bytes 8654848 | tf_op jit(solution)/shard_map/qhij,qihd->qjhd/dot_general | solution.py:82
  172.9 3.1 multiply_reduce_fusion
  176.0 5.4 %copy.40 = f32[1,1024,8,128]{3,2,1,0:T(8,128)} copy(f32[1,1024,8,128]{1,3,2,0:T(8,128)} %convolution_bitcast_fusion.1) | data formatting | bytes 8388608 | tf_op jit(solution)/shard_map/qhij,qihd->qjhd/transpose | solution.py:82
  181.3 4.9 %stack.34 = f32[1,1,8,131072]{3,2,1,0:T(8,128)} reshape(f32[1,1024,8,128]{3,2,1,0:T(8,128)} %copy.40) | data formatting | bytes 8388608 | tf_op jit(solution)/shard_map/stack | solution.py:100
  186.2 4.2 multiply_convert_fusion
  190.4 0.7 convolution_bitcast_fusion.2
  191.1 0.6 copy-done.1
  191.7 4.4 %copy.37 = f32[1,1024,8,128]{3,2,1,0:T(8,128)} copy(f32[1,1024,8,128]{3,1,2,0:T(8,128)S(1)} %convolution_bitcast_fusion.2) | data formatting | bytes 8388608 | tf_op jit(solution)/shard_map/qhij,qihd->qjhd/transpose | solution.py:93
  196.1 4.9 %stack.33 = f32[1,1,8,131072]{3,2,1,0:T(8,128)} reshape(f32[1,1024,8,128]{3,2,1,0:T(8,128)} %copy.37) | data formatting | bytes 8388608 | tf_op jit(solution)/shard_map/stack | solution.py:100
  201.0 5.7 %fusion.10 = f32[2,131072,2]{1,2,0:T(2,128)} fusion(f32[1,1,8,131072]{3,2,0,1:T(8,128)} %bitcast.138, f32[1,1,8,131072]{3,2,0,1:T(8,128)} %bitcast.140), kind=kLoop, calls=%fused_computation.23 | loop fusion | flops 524288 | bytes 10485760 | tf_op jit(solution)/shard_map/gj,kgx->kjx/dot_general | solution.py:179
  206.7 4.0 dot_general.56
  210.8 0.3 reduce-scatter.2.cloned.1.call-start
  211.0 3.6 convolution_convert_fusion.2
  214.6 4.5 %fusion.38 = f32[1024,2048]{1,0:T(8,128)} fusion(bf16[128,1024]{0,1:T(8,128)(2,1)S(1)} %bitcast.147, bf16[128,2048]{1,0:T(8,128)(2,1)S(1)} %copy-done), kind=kOutput, calls=%fused_computation.75 | convolution fusion | flops 536870912 | bytes 9175040 | tf_op jit(solution)/shard_map/dot_general | solution.py:157
  219.1 0.6 copy-done.10
  219.8 2.3 convolution_convert_fusion.1
  222.1 0.9 copy.43
  223.0 9.7 %convolution_bitcast_fusion = f32[2,3,131072]{2,1,0:T(4,128)} fusion(f32[1,1,8,131072]{3,2,0,1:T(8,128)} %bitcast.139, f32[1,1,8,131072]{3,2,0,1:T(8,128)} %bitcast.141, s32[6]{0:T(128)S(1)} %add_bitcast_fusion), kind=kOutput, calls=%fused_computation.2 | convolution fusion | flops 58195984 | bytes 11534360 | tf_op jit(solution)/shard_map/sj,ksx->kjx/dot_general | solution.py:110
  232.7 5.1 %reshape.362 = f32[2,384,1024]{2,1,0:T(8,128)} reshape(f32[2,3,131072]{2,1,0:T(4,128)} %convolution_bitcast_fusion) | data formatting | bytes 6291456 | tf_op jit(solution)/shard_map/reshape | solution.py:111
  237.8 2.3 convert.6
  240.2 1.3 collective-permute-start.3
  241.5 3.3 collective-permute-start.2
  244.9 1.5 convolution_convert_fusion
  246.4 67.3 %all-reduce.4.cloned.1.call-done = f32[2,128,1024,2]{2,1,3,0:T(8,128)} async-done(((f32[2,128,1024,2]{2,1,3,0:T(8,128)}), f32[2,128,1024,2]{2,1,3,0:T(8,128)}) %all-reduce.4.cloned.1.call-update) | async-done | bytes 2097168 | tf_op jit(solution)/shard_map/psum | solution.py:174
  313.7 6.6 %fusion.13 = f32[1,2,128,1024]{3,0,2,1:T(1,128)S(1)} fusion(f32[2,128,1024,2]{2,1,3,0:T(8,128)} %all-reduce.4.cloned.1.call-done, s32[2]{0:T(128)S(1)} %copy-done.8, s32[]{:T(128)S(6)} %axis_index.8), kind=kOutput, calls=%fused_computation.28 | convolution fusion | flops 6291458 | bytes 3145740 | tf_op jit(solution)/shard_map/gj,kgx->kjx/dot_general | solution.py:179
  320.3 1.7 fusion.18
  322.0 0.8 slice_bitcast_fusion
  322.8 99.8 %reduce-scatter.2.cloned.1.call-done = f32[64,2048]{1,0:T(8,128)} async-done(((f32[1024,2048]{1,0:T(8,128)}), f32[64,2048]{1,0:T(8,128)}) %reduce-scatter.2.cloned.1.call-update) | async-done | bytes 524304 | tf_op jit(solution)/shard_map/reduce_scatter | solution.py:156
  (48 shorter events, 0.9 us)
Async XLA Ops:
  7.2 156.8 %copy-start = (bf16[128,2048]{1,0:T(8,128)(2,1)S(1)}, bf16[128,2048]{1,0:T(8,128)(2,1)}, u32[]{:S(2)}) copy-start(bf16[128,2048]{1,0:T(8,128)(2,1)} %param.12) | copy-start | bytes 1572868
  7.2 10.8 %copy-start.12 = (s32[1,3,1]{1,2,0:T(1,128)S(1)}, s32[1,3,1]{1,2,0:T(1,128)}, u32[]{:S(2)}) copy-start(s32[1,3,1]{1,2,0:T(1,128)} %constant.63) | copy-start | bytes 40
  7.2 10.9 %copy-start.11 = (s32[3]{0:T(128)S(1)}, s32[3]{0:T(128)}, u32[]{:S(2)}) copy-start(s32[3]{0:T(128)} %constant.60.clone) | copy-start | bytes 40
  7.2 11.7 %copy-start.6 = (bf16[128,1024]{1,0:T(8,128)(2,1)S(1)}, bf16[128,1024]{1,0:T(8,128)(2,1)}, u32[]{:S(2)}) copy-start(bf16[128,1024]{1,0:T(8,128)(2,1)} %param.10) | copy-start | bytes 786436
  7.2 11.7 %copy-start.7 = (bf16[128,1024]{1,0:T(8,128)(2,1)S(1)}, bf16[128,1024]{1,0:T(8,128)(2,1)}, u32[]{:S(2)}) copy-start(bf16[128,1024]{1,0:T(8,128)(2,1)} %param.9) | copy-start | bytes 786436
  7.2 10.8 %copy-start.9 = (s32[1,3]{1,0:T(1,128)S(1)}, s32[1,3]{1,0:T(1,128)}, u32[]{:S(2)}) copy-start(s32[1,3]{1,0:T(1,128)} %param.14) | copy-start | bytes 40
  7.2 104.7 %all-reduce.6.cloned.1.call-start = ((), (), s32[]{:S(2)}) async-start(), calls=%async_computation.4 | async-start | bytes 2097152 | tf_op jit(solution)/shard_map/psum | solution.py:27
  12.1 151.9 %all-gather.2.cloned.1.call-start = ((), (), s32[]{:S(2)}) async-start(), calls=%async_computation.1 | async-start | bytes 4456448 | tf_op jit(solution)/shard_map/all_gather | solution.py:142
  12.8 300.8 %all-reduce.4.cloned.1.call-start = ((), (), s32[]{:S(2)}) async-start(), calls=%async_computation.2 | async-start | bytes 4194304 | tf_op jit(solution)/shard_map/psum | solution.py:174
  12.9 5.5 %collective-permute-start.1 = (bf16[2,128,1024]{2,1,0:T(8,128)(2,1)S(1)}, bf16[2,128,1024]{2,1,0:T(8,128)(2,1)S(1)}, u32[]{:S(2)}, u32[]{:S(2)}) collective-permute-start(bf16[2,128,1024]{2,1,0:T(8,128)(2,1)S(1)} %get-tuple-element.25), channel_id=1, source_target_pairs={{1,0},{2,1},{3,2},{4,3},{5,4},{6,5},{7,6},{8,7},{9,8},{10,9},{11,1... | collective-permute-start | bytes 1572872 | tf_op jit(solution)/shard_map/ppermute | solution.py:20
  14.2 4.7 %collective-permute-start = (bf16[2,128,1024]{2,1,0:T(8,128)(2,1)S(1)}, bf16[2,128,1024]{2,1,0:T(8,128)(2,1)}, u32[]{:S(2)}, u32[]{:S(2)}) collective-permute-start(bf16[2,128,1024]{2,1,0:T(8,128)(2,1)S(1)} %get-tuple-element.25), channel_id=1, source_target_pairs={{0,1},{1,2},{2,3},{3,4},{4,5},{5,6},{6,7},{7,8},{8,9},{9,10},{10,1... | collective-permute-start | bytes 1572872 | tf_op jit(solution)/shard_map/ppermute | solution.py:19
  124.3 3.3 copy-start.5
  167.9 5.0 %copy-start.3 = (f32[8,128,1024]{1,2,0:T(8,128)S(1)}, f32[8,128,1024]{1,2,0:T(8,128)}, u32[]{:S(2)}) copy-start(f32[8,128,1024]{1,2,0:T(8,128)} %get-tuple-element.29) | copy-start | bytes 12582916
  167.9 5.0 %copy-start.4 = (bf16[1024,8,128]{0,2,1:T(8,128)(2,1)S(1)}, bf16[1024,8,128]{0,2,1:T(8,128)(2,1)}, u32[]{:S(2)}) copy-start(bf16[1024,8,128]{0,2,1:T(8,128)(2,1)} %copy.52) | copy-start | bytes 6291460
  190.4 1.4 copy-start.1
  210.8 211.8 %reduce-scatter.2.cloned.1.call-start = ((), (), s32[]{:S(2)}) async-start(), calls=%async_computation.3 | async-start | bytes 8912896 | tf_op jit(solution)/shard_map/reduce_scatter | solution.py:156
  219.1 0.7 copy-start.10
  237.8 7.0 %copy-start.2 = (bf16[1024,2048]{1,0:T(8,128)(2,1)S(1)}, bf16[1024,2048]{1,0:T(8,128)(2,1)}, u32[]{:S(2)}) copy-start(bf16[1024,2048]{1,0:T(8,128)(2,1)} %all-gather.2.cloned.1.call-done) | copy-start | bytes 12582916
  240.1 73.6 %copy-start.8 = (s32[2]{0:T(128)S(1)}, s32[2]{0:T(128)}, u32[]{:S(2)}) copy-start(s32[2]{0:T(128)} %param.13) | copy-start | bytes 28
  240.2 80.0 %collective-permute-start.3 = (bf16[2,128,1024]{2,1,0:T(8,128)(2,1)S(1)}, bf16[2,128,1024]{2,1,0:T(8,128)(2,1)S(1)}, u32[]{:S(2)}, u32[]{:S(2)}) collective-permute-start(bf16[2,128,1024]{2,1,0:T(8,128)(2,1)S(1)} %get-tuple-element.20), channel_id=1, source_target_pairs={{1,0},{2,1},{3,2},{4,3},{5,4},{6,5},{7,6},{8,7},{9,8},{10,9},{11,1... | collective-permute-start | bytes 1572872 | tf_op jit(solution)/shard_map/ppermute | solution.py:20
  241.5 78.8 %collective-permute-start.2 = (bf16[2,128,1024]{2,1,0:T(8,128)(2,1)S(1)}, bf16[2,128,1024]{2,1,0:T(8,128)(2,1)S(1)}, u32[]{:S(2)}, u32[]{:S(2)}) collective-permute-start(bf16[2,128,1024]{2,1,0:T(8,128)(2,1)S(1)} %get-tuple-element.19), channel_id=1, source_target_pairs={{0,1},{1,2},{2,3},{3,4},{4,5},{5,6},{6,7},{7,8},{8,9},{9,10},{10,1... | collective-permute-start | bytes 1572872 | tf_op jit(solution)/shard_map/ppermute | solution.py:19
Sparse Core Ops, SparseCore 0:
  12.2 99.7 all-reduce.5
  114.1 49.8 all-gather.1
  210.9 102.7 all-reduce.3
  318.7 103.8 reduce-scatter.1
where the time goes:
time: 430 us; the launch traced here: 429 us
  waiting for transfers between devices  290 us (67%)
  local copies, waits for them, and re-layouts  46.4 us (11%)
  matrix products  41.4 us (10%)
  other arithmetic  26 us (6%)
  between operations  15.3 us (4%)
  starting transfers between devices  10.1 us (2%)
    reduce_scatter x1, waiting for transfers between devices, local(): lax.psum_scatter(lax.dot_general(columns, grad_out, (((0,), (0,)), ((), (...  99.8 us
    psum x1, waiting for transfers between devices, spread(): return lax.psum(jnp.where(mine, shard, jnp.zeros_like(shard)), axis)  89.4 us
    psum x1, waiting for transfers between devices, local(): global_total = lax.psum(grad_global, 'seq')  67.3 us
    all_gather x1, waiting for transfers between devices, local(): lax.all_gather(out_weight, 'seq', axis=0, tiled=True)  32.2 us
    another operation x2, local copies, waits for them, and re-layouts, fold_gradients(): stacked = jnp.stack([grad_chosen_keys, grad_chosen_values])  9.74 us
    dot_general x1, matrix products, fold_gradients(): jnp.einsum('sj,ksx->kjx', one_hot, local_part, precision=lax.Precision.HI...  9.71 us
  transfers between devices with their start and end apart: 8, of which 5 were waited for; matrix products, arithmetic and copies ran while one was open for 15% of the time, Pallas kernels for 0%

commit v1 on v0

--- a/solution.py
+++ b/solution.py
@@ -1,3 +1,4 @@
+import functools
 import math
 import jax
 import jax.numpy as jnp
@@ -7,6 +8,26 @@
 H = 8
 BLK = 128
 NEG_FILL = -1e30
+
+
+def layers_all_open(base_x, axis_no):
+    row_out, now, a_now = (lax.axis_size("seq"), lax.axis_index("seq"), base_x.shape[axis_no])
+    r2, t1 = (base_x, 1)
+    while t1 < row_out:
+        r2 = jnp.concatenate(
+            [
+                r2,
+                lax.ppermute(
+                    r2, "seq", tuple(((dd, (dd - t1) % row_out) for dd in range(row_out)))
+                ),
+            ],
+            axis=axis_no,
+        )
+        t1 = 2 * t1
+    return jnp.roll(r2, now * a_now, axis=axis_no)
+
+
+make_target_by_axis = functools.partial(layers_all_open, axis_no=0)
 
 
 def extended_2(shard, sides, width):
@@ -138,9 +159,7 @@
     attn_out = mixed_out.reshape(tok_rows, feature_count)
     columns = attn_out
     layer_sum = jnp.dot(
-        columns,
-        lax.all_gather(out_weight, "seq", axis=0, tiled=True),
-        preferred_element_type=jnp.float32,
+        columns, make_target_by_axis(out_weight), preferred_element_type=jnp.float32
     )
     upstream_sum = lax.dot_general(
         grad_out,

time: 430 us -> 525 us (1.22)
  waiting for transfers between devices: 290 us -> 368 us
  local copies, waits for them, and re-layouts: 46.4 us -> 59.7 us
  matrix products: 41.4 us -> 36 us
    ppermute x0 -> x4, waiting for transfers between devices: none -> 141 us  [layers_all_open(): lax.ppermute(r2, 'seq', tuple(((dd, (dd - t1) % row_out) for dd in range(...]
    psum x1, waiting for transfers between devices: 67.3 us -> 7.39 us  [local(): global_total = lax.psum(grad_global, 'seq')]
    unnamed x29 -> x48, local copies, waits for them, and re-layouts: 6.39 us -> 15.6 us
    ppermute x0 -> x4, starting transfers between devices: none -> 6.64 us  [layers_all_open(): lax.ppermute(r2, 'seq', tuple(((dd, (dd - t1) % row_out) for dd in range(...]
  transfers between devices with their start and end apart: 8 -> 12, of which waited for: 5 -> 8; matrix products, arithmetic and copies ran while one was open for 15% -> 14% of each run, Pallas kernels for 0% -> 0%
where the time goes in v1:
time: 525 us; the launch traced here: 524 us
  waiting for transfers between devices  368 us (70%)
  local copies, waits for them, and re-layouts  59.7 us (11%)
  matrix products  36 us (7%)
  other arithmetic  30.4 us (6%)
  between operations  15.4 us (3%)
  starting transfers between devices  14 us (3%)
    ppermute x4, waiting for transfers between devices, layers_all_open(): lax.ppermute(r2, 'seq', tuple(((dd, (dd - t1) % row_out) for dd in range(...  141 us
    reduce_scatter x1, waiting for transfers between devices, local(): lax.psum_scatter(lax.dot_general(columns, grad_out, (((0,), (0,)), ((), (...  101 us
    psum x1, waiting for transfers between devices, spread(): return lax.psum(jnp.where(mine, shard, jnp.zeros_like(shard)), axis)  88.4 us
    all_gather x1, waiting for transfers between devices, local(): lax.all_gather(out_weight, 'seq', axis=0, tiled=True)  29.8 us
    unnamed x48, local copies, waits for them, and re-layouts  15.6 us
  transfers between devices with their start and end apart: 12, of which 8 were waited for; matrix products, arithmetic and copies ran while one was open for 14% of the time, Pallas kernels for 0%

profile of v1, /device:TPU:0, one launch (start us, length us, event | category | flops | bytes accessed | tf_op | source)
XLA Modules:
  0.0 523.8 jit_solution(12936342039565399457)
XLA Ops:
  7.2 1.3 fusion.42
  9.8 2.1 select_bitcast_fusion.1
  12.8 1.3 collective-permute-start.1
  14.1 3.1 collective-permute-start
  21.3 2.5 gather_fusion
  23.8 88.4 %all-reduce.6.cloned.1.call-done = (bf16[1,2,128,1024]{3,2,1,0:T(8,128)(2,1)}, bf16[1,2,128,1024]{3,2,1,0:T(8,128)(2,1)}) async-done(((bf16[1,2,128,1024]{3,2,1,0:T(8,128)(2,1)}, bf16[1,2,128,1024]{3,2,1,0:T(8,128)(2,1)}), (bf16[1,2,128,1024]{3,2,1,0:T(8,128)(2,1)}, bf16[1,2,128,1024]{3,2,1,0:T(8,128)(2,1)})) %all-reduce.6.cloned.1.call-update) | async-done | bytes 1048592 | tf_op jit(solution)/shard_map/psum | solution.py:48
  112.2 1.3 maximum_bitcast_fusion.2
  113.5 2.3 bitcast_select_fusion
  115.8 1.5 pad_maximum_fusion.1
  117.3 1.9 copy.58
  119.3 3.3 copy.34
  122.5 3.6 copy.57
  126.1 4.2 copy.52
  131.1 3.4 fusion.43
  134.5 29.8 %all-gather.2.cloned.1.call-done = bf16[1024,2048]{1,0:T(8,128)(2,1)} async-done(((bf16[64,2048]{1,0:T(8,128)(2,1)}), bf16[1024,2048]{1,0:T(8,128)(2,1)}) %all-gather.2.cloned.1.call-update) | async-done | bytes 4194320 | tf_op jit(solution)/shard_map/all_gather | solution.py:166
  164.3 3.7 convolution_convert_fusion.2
  168.2 5.1 convolution_bitcast_fusion.1
  173.2 3.1 multiply_reduce_fusion
  176.3 5.4 %copy.40 = f32[1,1024,8,128]{3,2,1,0:T(8,128)} copy(f32[1,1024,8,128]{1,3,2,0:T(8,128)} %convolution_bitcast_fusion.1) | data formatting | bytes 8388608 | tf_op jit(solution)/shard_map/qhij,qihd->qjhd/transpose | solution.py:103
  181.7 4.9 stack.34
  186.6 4.2 multiply_convert_fusion
  190.8 1.3 copy-done.3
  192.8 4.5 copy.37
  197.3 4.9 stack.33
  202.2 5.7 %fusion.15 = f32[2,131072,2]{1,2,0:T(2,128)} fusion(f32[1,1,8,131072]{3,2,0,1:T(8,128)} %bitcast.137, f32[1,1,8,131072]{3,2,0,1:T(8,128)} %bitcast.139), kind=kLoop, calls=%fused_computation.25 | loop fusion | flops 524288 | bytes 10485760 | tf_op jit(solution)/shard_map/gj,kgx->kjx/dot_general | solution.py:198
  207.9 4.0 dot_general.56
  212.0 3.5 convolution_convert_fusion.1
  216.2 4.5 fusion.44
  221.7 1.7 collective-permute-start.2
  223.4 7.2 %collective-permute-done.2 = bf16[64,2048]{1,0:T(8,128)(2,1)S(1)} collective-permute-done((bf16[64,2048]{1,0:T(8,128)(2,1)S(1)}, bf16[64,2048]{1,0:T(8,128)(2,1)S(1)}, u32[]{:S(2)}, u32[]{:S(2)}) %collective-permute-start.2) | collective-permute-done | bytes 262176 | tf_op jit(solution)/shard_map/ppermute | solution.py:20
  230.7 15.5 %collective-permute-done.3 = bf16[128,2048]{1,0:T(8,128)(2,1)S(1)} collective-permute-done((bf16[128,2048]{1,0:T(8,128)(2,1)S(1)}, bf16[128,2048]{1,0:T(8,128)(2,1)S(1)}, u32[]{:S(2)}, u32[]{:S(2)}) %collective-permute-start.3) | collective-permute-done | bytes 524320 | tf_op jit(solution)/shard_map/ppermute | solution.py:20
  246.2 1.8 collective-permute-start.4
  248.0 26.7 %collective-permute-done.4 = bf16[256,2048]{1,0:T(8,128)(2,1)S(1)} collective-permute-done((bf16[256,2048]{1,0:T(8,128)(2,1)S(1)}, bf16[256,2048]{1,0:T(8,128)(2,1)S(1)}, u32[]{:S(2)}, u32[]{:S(2)}) %collective-permute-start.4) | collective-permute-done | bytes 1048608 | tf_op jit(solution)/shard_map/ppermute | solution.py:20
  275.7 1.5 pad_maximum_fusion.2
  277.2 3.1 collective-permute-start.5
  281.5 1.4 constant_dynamic-update-slice_fusion.6
  282.9 91.5 %collective-permute-done.5 = bf16[512,2048]{1,0:T(8,128)(2,1)} collective-permute-done((bf16[512,2048]{1,0:T(8,128)(2,1)}, bf16[512,2048]{1,0:T(8,128)(2,1)}, u32[]{:S(2)}, u32[]{:S(2)}) %collective-permute-start.5) | collective-permute-done | bytes 2097184 | tf_op jit(solution)/shard_map/ppermute | solution.py:20
  374.5 1.8 constant_dynamic-update-slice_fusion.5
  376.5 2.0 constant_dynamic-update-slice_fusion
  378.5 1.5 fusion.11
  380.8 5.7 %convolution_bitcast_fusion = f32[2,3,131072]{2,1,0:T(4,128)} fusion(f32[1,1,8,131072]{3,2,0,1:T(8,128)S(1)} %bitcast.138, f32[1,1,8,131072]{3,2,0,1:T(8,128)S(1)} %bitcast.140, s32[6]{0:T(128)S(1)} %add_bitcast_fusion), kind=kOutput, calls=%fused_computation.2 | convolution fusion | flops 58195984 | bytes 11534360 | tf_op jit(solution)/shard_map/sj,ksx->kjx/dot_general | solution.py:131
  386.5 5.1 reshape.362
  391.7 2.3 convert.6
  395.1 1.5 collective-permute-start.6
  399.6 7.4 %all-reduce.4.cloned.1.call-done = f32[2,128,1024,2]{2,1,3,0:T(8,128)} async-done(((f32[2,128,1024,2]{2,1,3,0:T(8,128)}), f32[2,128,1024,2]{2,1,3,0:T(8,128)}) %all-reduce.4.cloned.1.call-update) | async-done | bytes 2097168 | tf_op jit(solution)/shard_map/psum | solution.py:193
  407.0 6.6 %fusion.18 = f32[1,2,128,1024]{3,0,2,1:T(1,128)S(1)} fusion(f32[2,128,1024,2]{2,1,3,0:T(8,128)} %all-reduce.4.cloned.1.call-done, s32[2]{0:T(128)S(1)} %copy-done.15, s32[]{:T(128)S(6)} %axis_index.8), kind=kOutput, calls=%fused_computation.31 | convolution fusion | flops 6291458 | bytes 3145740 | tf_op jit(solution)/shard_map/gj,kgx->kjx/dot_general | solution.py:198
  413.6 1.8 fusion.23
  416.2 101.0 %reduce-scatter.2.cloned.1.call-done = f32[64,2048]{1,0:T(8,128)} async-done(((f32[1024,2048]{1,0:T(8,128)}), f32[64,2048]{1,0:T(8,128)}) %reduce-scatter.2.cloned.1.call-update) | async-done | bytes 524304 | tf_op jit(solution)/shard_map/reduce_scatter | solution.py:175
  (79 shorter events, 16.4 us)
Async XLA Ops:
  7.2 157.1 %copy-start = (bf16[128,2048]{1,0:T(8,128)(2,1)S(1)}, bf16[128,2048]{1,0:T(8,128)(2,1)}, u32[]{:S(2)}) copy-start(bf16[128,2048]{1,0:T(8,128)(2,1)} %param.12) | copy-start | bytes 1572868
  7.2 105.0 %all-reduce.6.cloned.1.call-start = ((), (), s32[]{:S(2)}) async-start(), calls=%async_computation.4 | async-start | bytes 2097152 | tf_op jit(solution)/shard_map/psum | solution.py:48
  12.0 152.3 %all-gather.2.cloned.1.call-start = ((), (), s32[]{:S(2)}) async-start(), calls=%async_computation.1 | async-start | bytes 4456448 | tf_op jit(solution)/shard_map/all_gather | solution.py:166
  12.7 394.2 %all-reduce.4.cloned.1.call-start = ((), (), s32[]{:S(2)}) async-start(), calls=%async_computation.2 | async-start | bytes 4194304 | tf_op jit(solution)/shard_map/psum | solution.py:193
  12.8 7.3 %collective-permute-start.1 = (bf16[2,128,1024]{2,1,0:T(8,128)(2,1)S(1)}, bf16[2,128,1024]{2,1,0:T(8,128)(2,1)S(1)}, u32[]{:S(2)}, u32[]{:S(2)}) collective-permute-start(bf16[2,128,1024]{2,1,0:T(8,128)(2,1)S(1)} %get-tuple-element.25), channel_id=1, source_target_pairs={{1,0},{2,1},{3,2},{4,3},{5,4},{6,5},{7,6},{8,7},{9,8},{10,9},{11,1... | collective-permute-start | bytes 1572872 | tf_op jit(solution)/shard_map/ppermute | solution.py:41
  14.1 6.0 %collective-permute-start = (bf16[2,128,1024]{2,1,0:T(8,128)(2,1)S(1)}, bf16[2,128,1024]{2,1,0:T(8,128)(2,1)S(1)}, u32[]{:S(2)}, u32[]{:S(2)}) collective-permute-start(bf16[2,128,1024]{2,1,0:T(8,128)(2,1)S(1)} %get-tuple-element.25), channel_id=1, source_target_pairs={{0,1},{1,2},{2,3},{3,4},{4,5},{5,6},{6,7},{7,8},{8,9},{9,10},{10,1... | collective-permute-start | bytes 1572872 | tf_op jit(solution)/shard_map/ppermute | solution.py:40
  122.5 7.8 %copy-start.14 = (bf16[128,1024]{1,0:T(8,128)(2,1)S(1)}, bf16[128,1024]{1,0:T(8,128)(2,1)}, u32[]{:S(2)}) copy-start(bf16[128,1024]{1,0:T(8,128)(2,1)} %param.8) | copy-start | bytes 786436
  168.2 5.1 copy-start.10
  168.2 5.1 copy-start.11
  190.8 1.3 copy-start.3
  211.9 305.3 %reduce-scatter.2.cloned.1.call-start = ((), (), s32[]{:S(2)}) async-start(), calls=%async_computation.3 | async-start | bytes 8912896 | tf_op jit(solution)/shard_map/reduce_scatter | solution.py:175
  215.5 0.7 copy-start.12
  220.7 1.0 copy-start.7
  221.7 58.6 %copy-start.16 = (s32[1,3]{1,0:T(1,128)S(1)}, s32[1,3]{1,0:T(1,128)}, u32[]{:S(2)}) copy-start(s32[1,3]{1,0:T(1,128)} %param.14) | copy-start | bytes 40
  221.7 58.6 %copy-start.17 = (s32[1,3]{1,0:T(1,128)S(1)}, s32[1,3]{1,0:T(1,128)}, u32[]{:S(2)}) copy-start(s32[1,3]{1,0:T(1,128)} %constant.87) | copy-start | bytes 40
  221.7 8.9 %collective-permute-start.2 = (bf16[64,2048]{1,0:T(8,128)(2,1)S(1)}, bf16[64,2048]{1,0:T(8,128)(2,1)S(1)}, u32[]{:S(2)}, u32[]{:S(2)}) collective-permute-start(bf16[64,2048]{1,0:T(8,128)(2,1)S(1)} %copy-done.7), channel_id=1, source_target_pairs={{0,15},{1,0},{2,1},{3,2},{4,3},{5,4},{6,5},{7,6},{8,7},{9,8},{10,9... | collective-permute-start | bytes 786440 | tf_op jit(solution)/shard_map/ppermute | solution.py:20
  230.6 46.6 %copy-start.8 = (bf16[64,2048]{1,0:T(8,128)(2,1)}, bf16[64,2048]{1,0:T(8,128)(2,1)S(1)}, u32[]{:S(2)}) copy-start(bf16[64,2048]{1,0:T(8,128)(2,1)S(1)} %collective-permute-done.2) | copy-start | bytes 786436
  230.6 15.5 %collective-permute-start.3 = (bf16[128,2048]{1,0:T(8,128)(2,1)S(1)}, bf16[128,2048]{1,0:T(8,128)(2,1)S(1)}, u32[]{:S(2)}, u32[]{:S(2)}) collective-permute-start(bf16[128,2048]{1,0:T(8,128)(2,1)S(1)} %pad_maximum_fusion.6), channel_id=1, source_target_pairs={{0,14},{1,15},{2,0},{3,1},{4,2},{5,3},{6,4},{7,5},{8,6},{9,7},{10,... | collective-permute-start | bytes 1572872 | tf_op jit(solution)/shard_map/ppermute | solution.py:20
  246.2 28.5 %collective-permute-start.4 = (bf16[256,2048]{1,0:T(8,128)(2,1)S(1)}, bf16[256,2048]{1,0:T(8,128)(2,1)S(1)}, u32[]{:S(2)}, u32[]{:S(2)}) collective-permute-start(bf16[256,2048]{1,0:T(8,128)(2,1)S(1)} %pad_maximum_fusion.4), channel_id=1, source_target_pairs={{0,12},{1,13},{2,14},{3,15},{4,0},{5,1},{6,2},{7,3},{8,4},{9,5},{1... | collective-permute-start | bytes 3145736 | tf_op jit(solution)/shard_map/ppermute | solution.py:20
  274.7 1.0 copy-start.5
  277.2 97.3 %collective-permute-start.5 = (bf16[512,2048]{1,0:T(8,128)(2,1)}, bf16[512,2048]{1,0:T(8,128)(2,1)}, u32[]{:S(2)}, u32[]{:S(2)}) collective-permute-start(bf16[512,2048]{1,0:T(8,128)(2,1)} %pad_maximum_fusion.2), channel_id=1, source_target_pairs={{0,8},{1,9},{2,10},{3,11},{4,12},{5,13},{6,14},{7,15},{8,0},{9,1},... | collective-permute-start | bytes 6291464 | tf_op jit(solution)/shard_map/ppermute | solution.py:20
  280.4 95.9 %copy-start.9 = (bf16[64,2048]{1,0:T(8,128)(2,1)S(1)}, bf16[64,2048]{1,0:T(8,128)(2,1)}, u32[]{:S(2)}) copy-start(bf16[64,2048]{1,0:T(8,128)(2,1)} %copy-done.8) | copy-start | bytes 786436
  281.5 94.9 %copy-start.6 = (bf16[256,2048]{1,0:T(8,128)(2,1)S(1)}, bf16[256,2048]{1,0:T(8,128)(2,1)}, u32[]{:S(2)}) copy-start(bf16[256,2048]{1,0:T(8,128)(2,1)} %copy-done.5) | copy-start | bytes 3145732
  376.3 2.2 copy-start.13
  376.5 3.6 copy-start.1
  376.5 4.3 copy-start.2
  391.7 6.3 %copy-start.4 = (bf16[8,128,1024]{1,2,0:T(8,128)(2,1)S(1)}, bf16[8,128,1024]{1,2,0:T(8,128)(2,1)}, u32[]{:S(2)}) copy-start(bf16[8,128,1024]{1,2,0:T(8,128)(2,1)} %copy-done.3) | copy-start | bytes 6291460
  394.0 13.0 %copy-start.15 = (s32[2]{0:T(128)S(1)}, s32[2]{0:T(128)}, u32[]{:S(2)}) copy-start(s32[2]{0:T(128)} %param.13) | copy-start | bytes 28
  395.1 18.4 %collective-permute-start.6 = (bf16[2,128,1024]{2,1,0:T(8,128)(2,1)}, bf16[2,128,1024]{2,1,0:T(8,128)(2,1)S(1)}, u32[]{:S(2)}, u32[]{:S(2)}) collective-permute-start(bf16[2,128,1024]{2,1,0:T(8,128)(2,1)} %get-tuple-element.19), channel_id=1, source_target_pairs={{0,1},{1,2},{2,3},{3,4},{4,5},{5,6},{6,7},{7,8},{8,9},{9,10},{10,1... | collective-permute-start | bytes 1572872 | tf_op jit(solution)/shard_map/ppermute | solution.py:40
  396.7 16.9 %collective-permute-start.7 = (bf16[2,128,1024]{2,1,0:T(8,128)(2,1)}, bf16[2,128,1024]{2,1,0:T(8,128)(2,1)}, u32[]{:S(2)}, u32[]{:S(2)}) collective-permute-start(bf16[2,128,1024]{2,1,0:T(8,128)(2,1)} %get-tuple-element.20), channel_id=1, source_target_pairs={{1,0},{2,1},{3,2},{4,3},{5,4},{6,5},{7,6},{8,7},{9,8},{10,9},{11,1... | collective-permute-start | bytes 1572872 | tf_op jit(solution)/shard_map/ppermute | solution.py:41
Sparse Core Ops, SparseCore 0:
  12.1 100.0 all-reduce.5
  114.4 49.8 all-gather.1
  212.0 194.8 all-reduce.3
  412.0 105.1 reduce-scatter.1
